TPU v7x, 512 devices: a whole 4x8x8 slice. The times are simulated.
512 devices in a mesh: exp: 128 (over y, z, core), hid: 4 (over x).
Axes of the slice: x: 4, y: 8, z: 8, core: 2. Of those that a mesh axis runs over, the one named last changes fastest.
Arguments:
- tokens: bfloat16 [4096, 4096], P('exp', 'hid'), may hold values from -6 to 6
- expert_ids: int32 [4096, 8], P('exp'), may hold values from 0 to 127, all different within a row; in each aligned block of 16 rows (0 to 15, 16 to 31, ...) at most 2 rows name the same one
- combine: float32 [4096, 8], P('exp'), may hold values from 0.05 to 0.4
- sign_bits: int32 [128, 768], P('exp'), may hold values from 0 to 1
- w_gate: bfloat16 [128, 768, 4096], P('exp', 'hid'), may hold values from -0.09375 to 0.09375
- w_up: bfloat16 [128, 768, 4096], P('exp', 'hid'), may hold values from -0.09375 to 0.09375
- w_down: bfloat16 [128, 768, 4096], P('exp', 'hid'), may hold values from -0.21875 to 0.21875
Outputs:
- next_input: bfloat16 [4096, 4096], P('exp', 'hid')
- hessian: bfloat16 [128, 768, 768], P('exp', 'hid')
Inputs may be any that keep to these rules, and one draw needn't show every extreme that they name: `expert_ids`: each row names 8 different experts. Within each aligned block of 16 rows (one micro-batch of one index of exp) no expert is named by more than 2 rows, a bound that some block reaches. `sign_bits`: 0 stands for the sign -1, 1 for +1.
All inputs are finite; a program needn't handle non-finite values.
Results may differ from a plain program's by a relative error of at most 0.0065.
Values may be sent and summed in bfloat16 or wider, within the bound.
No kernel may reach another device: no remote copies, remote signals or barrier semaphores. Data moves between devices by JAX's collectives and lax.ppermute only.
A program may use at most 64 MiB of HBM per device.

v0:
```python
import jax
import jax.numpy as jnp
import numpy as np
from jax import lax
from jax.sharding import PartitionSpec as P


def paley_twelve():
    residues = set((number * number % 11 for number in range(1, 11)))
    legendre = [0] + [1 if number in residues else -1 for number in range(1, 11)]
    hadamard = np.zeros((12, 12))
    hadamard[0, 1:] = 1.0
    hadamard[1:, 0] = -1.0
    for row_index in range(11):
        for col_index in range(11):
            hadamard[row_index + 1, col_index + 1] = legendre[(col_index - row_index) % 11]
    return hadamard + np.eye(12)


def sylvester(order_size):
    positions = jnp.arange(order_size, dtype=jnp.int32)
    common = positions[:, None] & positions[None, :]
    parity = jnp.zeros_like(common)
    for bit_pos in range(order_size.bit_length()):
        parity = parity + (common >> bit_pos & 1)
    return (1 - 2 * (parity % 2)).astype(jnp.float32)


def rotate(hidden, sign_rows, paley_table, sylvester_table):
    values = hidden.astype(jnp.float32) * jnp.expand_dims(sign_rows, -2)
    blocks = values.reshape(values.shape[:-1] + (12, sylvester_table.shape[0]))
    turned = jnp.einsum(
        "...ab,ca,db->...cd", blocks, paley_table, sylvester_table, precision=lax.Precision.HIGHEST
    )
    return turned.reshape(values.shape)


def rank_of_pick(ids_block, experts):
    flat_ids = ids_block.reshape(-1)
    onehot = (flat_ids[:, None] == jnp.arange(experts, dtype=jnp.int32)[None, :]).astype(jnp.int32)
    before = jnp.cumsum(onehot, axis=0) - onehot
    return jnp.sum(before * onehot, axis=1).reshape(ids_block.shape)


def shift_hid(value, shift, n_hid):
    return lax.ppermute(value, "hid", [(i, (i + shift) % n_hid) for i in range(n_hid)])


def layer(tokens, expert_ids, combine, sign_bits, w_gate, w_up, w_down):
    n_exp = lax.axis_size("exp")
    n_hid = lax.axis_size("hid")
    hid_index = lax.axis_index("hid")
    experts = w_gate.shape[0] * n_exp
    tok_rows, own_cols = tokens.shape
    half_rows = tok_rows // 2
    top_count = expert_ids.shape[1]
    capacity = min(half_rows, max(2, 2 * half_rows * top_count // experts))
    hidden_units = sign_bits.shape[1]
    share_rows = hidden_units // n_hid
    per_pair = 2 * capacity
    paley_table = jnp.asarray(paley_twelve(), jnp.float32)
    sylvester_table = sylvester(hidden_units // 12)
    sign_rows = (2 * sign_bits - 1).astype(jnp.float32)
    gram_scale = experts / (tok_rows * n_exp * top_count * hidden_units)
    shifts = range(n_hid)
    source = [(hid_index - s) % n_hid for s in shifts]
    down_pieces = [
        shift_hid(
            lax.dynamic_slice_in_dim(w_down[0], ((hid_index + s) % n_hid) * own_cols, own_cols, 1),
            s,
            n_hid,
        )
        if s
        else lax.dynamic_slice_in_dim(w_down[0], hid_index * own_cols, own_cols, 1)
        for s in shifts
    ]
    ranks = jnp.concatenate(
        [rank_of_pick(expert_ids[b * half_rows : (b + 1) * half_rows], experts) for b in range(2)],
        axis=0,
    )
    batch_of_row = (jnp.arange(tok_rows, dtype=jnp.int32) // half_rows)[:, None]
    target = expert_ids * per_pair + batch_of_row * capacity + ranks
    selector = jnp.any(
        target[None, :, :] == jnp.arange(experts * per_pair, dtype=jnp.int32)[:, None, None],
        axis=2,
    ).astype(jnp.bfloat16)
    sending = jnp.dot(selector, tokens, preferred_element_type=jnp.float32).astype(jnp.bfloat16)
    arrived = lax.all_to_all(sending, "exp", split_axis=0, concat_axis=0, tiled=True)
    in_pieces = [arrived]
    for s in shifts[1:]:
        in_pieces.append(shift_hid(arrived, s, n_hid))
    gate_act = sum(
        jnp.dot(
            in_pieces[s],
            lax.dynamic_slice_in_dim(w_gate[0], source[s] * own_cols, own_cols, 1).T,
            preferred_element_type=jnp.float32,
        )
        for s in shifts
    )
    up_act = sum(
        jnp.dot(
            in_pieces[s],
            lax.dynamic_slice_in_dim(w_up[0], source[s] * own_cols, own_cols, 1).T,
            preferred_element_type=jnp.float32,
        )
        for s in shifts
    )
    hidden = (jax.nn.silu(gate_act) * up_act).astype(jnp.bfloat16)
    hid_pieces = [shift_hid(hidden, s, n_hid) if s else hidden for s in shifts]
    out_cols = sum(
        jnp.dot(hid_pieces[s], down_pieces[s], preferred_element_type=jnp.float32) for s in shifts
    ).astype(jnp.bfloat16)
    back_rows = lax.all_to_all(out_cols, "exp", split_axis=0, concat_axis=0, tiled=True)
    picked = back_rows[target]
    mixed_rows = tokens.astype(jnp.float32) + jnp.sum(
        combine[:, :, None] * picked.astype(jnp.float32), axis=1
    )
    stacked = jnp.stack(hid_pieces)
    order = (hid_index - jnp.arange(n_hid, dtype=jnp.int32)) % n_hid
    full_hidden = jnp.take(stacked, order, axis=0).transpose(1, 0, 2).reshape(-1, hidden_units)
    rotated = rotate(full_hidden, sign_rows[0], paley_table, sylvester_table)
    own_rotated = lax.dynamic_slice_in_dim(rotated, hid_index * share_rows, share_rows, 1)
    gram = jnp.dot(own_rotated.T, rotated, precision=lax.Precision.HIGHEST)
    hessian = (gram * gram_scale).astype(jnp.bfloat16)
    return (mixed_rows.astype(jnp.bfloat16), hessian[None])


def solution(mesh):
    placed = (
        P("exp", "hid"),
        P("exp", None),
        P("exp", None),
        P("exp", None),
        P("exp", "hid", None),
        P("exp", "hid", None),
        P("exp", "hid", None),
    )
    return jax.shard_map(
        layer,
        mesh=mesh,
        in_specs=placed,
        out_specs=(P("exp", "hid"), P("exp", "hid", None)),
        check_vma=False,
    )
```

profile of v0, /device:TPU:1, one launch (start us, length us, event | category | flops | bytes accessed | tf_op | source)
XLA Modules:
  0.0 190.0 jit_solution(3542894795111833133)
XLA Ops:
  0.7 0.9 fusion.75
  1.8 0.2 reduce_window_sum.17
  2.0 0.2 select_reduce_fusion.1
  2.6 0.2 reduce_window_sum.18
  3.1 0.8 compare_select_fusion
  4.0 0.2 fusion.9
  4.2 1.3 convolution_convert_fusion
  5.5 1.2 all_to_all.16
  6.7 49.0 %all_to_all.24 = bf16[128,4,1024]{2,1,0:T(4,128)(2,1)} all-to-all(bf16[128,4,1024]{2,1,0:T(4,128)(2,1)} %all_to_all.16), channel_id=1, replica_groups=mesh['exp'=128,'hid'=4] {'exp'}, dimensions={0} | all-to-all | bytes 2097152 | tf_op jit(solution)/shard_map/all_to_all | solution.py:88
  55.7 1.3 all_to_all.18
  57.0 4.4 %collective-permute-start.2 = (bf16[512,1024]{1,0:T(8,128)(2,1)S(1)}, bf16[512,1024]{1,0:T(8,128)(2,1)}, u32[]{:S(2)}, u32[]{:S(2)}) collective-permute-start(bf16[512,1024]{1,0:T(8,128)(2,1)S(1)} %all_to_all.18), channel_id=1, source_target_pairs={{0,3},{1,0},{2,1},{3,2},{4,7},{5,4},{6,5},{7,6},{8,11},{9,8},{10,9... | collective-permute-start | bytes 3145736 | tf_op jit(solution)/shard_map/ppermute | solution.py:46
  61.5 1.9 %collective-permute-start = (bf16[512,1024]{1,0:T(8,128)(2,1)S(1)}, bf16[512,1024]{1,0:T(8,128)(2,1)}, u32[]{:S(2)}, u32[]{:S(2)}) collective-permute-start(bf16[512,1024]{1,0:T(8,128)(2,1)S(1)} %all_to_all.18), channel_id=1, source_target_pairs={{0,1},{1,2},{2,3},{3,0},{4,5},{5,6},{6,7},{7,4},{8,9},{9,10},{10,1... | collective-permute-start | bytes 3145736 | tf_op jit(solution)/shard_map/ppermute | solution.py:46
  63.4 2.3 %dynamic-slice_bitcast_fusion.2 = (bf16[192,1024]{1,0:T(8,128)(2,1)}, bf16[192,1024]{1,0:T(8,128)(2,1)}, bf16[192,1024]{1,0:T(8,128)(2,1)}) fusion(bf16[1,192,4096]{2,1,0:T(8,128)(2,1)} %param.14, s32[]{:T(128)S(6)} %select_n.130, s32[]{:T(128)S(6)} %select_n.134, s32[]{:T(128)S(6)} %select_n.132), kind=kLoop, calls=%fused_computation.41 | loop fusion | bytes 2359308 | tf_op jit(solution)/shard_map/dynamic_slice | solution.py:69
  65.7 2.1 %collective-permute-start.4 = (bf16[192,1024]{1,0:T(8,128)(2,1)}, bf16[192,1024]{1,0:T(8,128)(2,1)}, u32[]{:S(2)}, u32[]{:S(2)}) collective-permute-start(bf16[192,1024]{1,0:T(8,128)(2,1)} %get-tuple-element.4), channel_id=1, source_target_pairs={{0,1},{1,2},{2,3},{3,0},{4,5},{5,6},{6,7},{7,4},{8,9},{9,10},{10,1... | collective-permute-start | bytes 1179656 | tf_op jit(solution)/shard_map/ppermute | solution.py:46
  67.8 5.6 %collective-permute-start.6 = (bf16[192,1024]{1,0:T(8,128)(2,1)}, bf16[192,1024]{1,0:T(8,128)(2,1)}, u32[]{:S(2)}, u32[]{:S(2)}) collective-permute-start(bf16[192,1024]{1,0:T(8,128)(2,1)} %get-tuple-element.6), channel_id=1, source_target_pairs={{0,2},{1,3},{2,0},{3,1},{4,6},{5,7},{6,4},{7,5},{8,10},{9,11},{10,... | collective-permute-start | bytes 1179656 | tf_op jit(solution)/shard_map/ppermute | solution.py:46
  73.4 1.9 %collective-permute-start.8 = (bf16[192,1024]{1,0:T(8,128)(2,1)}, bf16[192,1024]{1,0:T(8,128)(2,1)}, u32[]{:S(2)}, u32[]{:S(2)}) collective-permute-start(bf16[192,1024]{1,0:T(8,128)(2,1)} %get-tuple-element.5), channel_id=1, source_target_pairs={{0,3},{1,0},{2,1},{3,2},{4,7},{5,4},{6,5},{7,6},{8,11},{9,8},{10,9... | collective-permute-start | bytes 1179656 | tf_op jit(solution)/shard_map/ppermute | solution.py:46
  75.4 1.5 fusion.16
  76.9 0.5 fusion.22
  77.4 5.5 %collective-permute-done.2 = bf16[512,1024]{1,0:T(8,128)(2,1)} collective-permute-done((bf16[512,1024]{1,0:T(8,128)(2,1)S(1)}, bf16[512,1024]{1,0:T(8,128)(2,1)}, u32[]{:S(2)}, u32[]{:S(2)}) %collective-permute-start.2) | collective-permute-done | bytes 1048608 | tf_op jit(solution)/shard_map/ppermute | solution.py:46
  82.9 3.7 %collective-permute-start.1 = (bf16[512,1024]{1,0:T(8,128)(2,1)S(1)}, bf16[512,1024]{1,0:T(8,128)(2,1)S(1)}, u32[]{:S(2)}, u32[]{:S(2)}) collective-permute-start(bf16[512,1024]{1,0:T(8,128)(2,1)S(1)} %all_to_all.18), channel_id=1, source_target_pairs={{0,2},{1,3},{2,0},{3,1},{4,6},{5,7},{6,4},{7,5},{8,10},{9,11},{10,... | collective-permute-start | bytes 3145736 | tf_op jit(solution)/shard_map/ppermute | solution.py:46
  86.6 1.7 fusion.18
  88.3 1.7 fusion.12
  90.1 1.7 convolution_add_fusion.1
  91.8 1.7 convolution_add_fusion.3
  93.6 32.1 %collective-permute-done.1 = bf16[512,1024]{1,0:T(8,128)(2,1)S(1)} collective-permute-done((bf16[512,1024]{1,0:T(8,128)(2,1)S(1)}, bf16[512,1024]{1,0:T(8,128)(2,1)S(1)}, u32[]{:S(2)}, u32[]{:S(2)}) %collective-permute-start.1) | collective-permute-done | bytes 1048608 | tf_op jit(solution)/shard_map/ppermute | solution.py:46
  125.6 0.5 fusion.4
  126.2 0.5 multiply_convert_fusion
  126.7 1.9 %collective-permute-start.3 = (bf16[512,192]{0,1:T(8,128)(2,1)S(1)}, bf16[512,192]{0,1:T(8,128)(2,1)S(1)}, u32[]{:S(2)}, u32[]{:S(2)}) collective-permute-start(bf16[512,192]{0,1:T(8,128)(2,1)S(1)} %multiply_convert_fusion), channel_id=1, source_target_pairs={{0,1},{1,2},{2,3},{3,0},{4,5},{5,6},{6,7},{7,4},{8,9},{9,10},{10,1... | collective-permute-start | bytes 589832 | tf_op jit(solution)/shard_map/ppermute | solution.py:46
  128.6 3.4 %collective-permute-start.5 = (bf16[512,192]{0,1:T(8,128)(2,1)S(1)}, bf16[512,192]{0,1:T(8,128)(2,1)S(1)}, u32[]{:S(2)}, u32[]{:S(2)}) collective-permute-start(bf16[512,192]{0,1:T(8,128)(2,1)S(1)} %multiply_convert_fusion), channel_id=1, source_target_pairs={{0,2},{1,3},{2,0},{3,1},{4,6},{5,7},{6,4},{7,5},{8,10},{9,11},{10,... | collective-permute-start | bytes 589832 | tf_op jit(solution)/shard_map/ppermute | solution.py:46
  132.0 1.5 fusion.10
  133.5 4.0 %collective-permute-start.7 = (bf16[512,192]{0,1:T(8,128)(2,1)S(1)}, bf16[512,192]{0,1:T(8,128)(2,1)S(1)}, u32[]{:S(2)}, u32[]{:S(2)}) collective-permute-start(bf16[512,192]{0,1:T(8,128)(2,1)S(1)} %multiply_convert_fusion), channel_id=1, source_target_pairs={{0,3},{1,0},{2,1},{3,2},{4,7},{5,4},{6,5},{7,6},{8,11},{9,8},{10,9... | collective-permute-start | bytes 589832 | tf_op jit(solution)/shard_map/ppermute | solution.py:46
  137.5 1.5 fusion.76
  139.1 1.5 fusion.77
  140.6 1.6 collective-permute-done.7
  142.3 1.5 add_convert_fusion
  143.8 1.2 all_to_all.19
  145.1 11.2 %all-to-all-start.1 = ((bf16[128,4,1024]{2,1,0:T(4,128)(2,1)}), bf16[128,4,1024]{2,1,0:T(4,128)(2,1)}, u32[]{:S(2)}, u32[]{:S(2)}) async-start(bf16[128,4,1024]{2,1,0:T(4,128)(2,1)} %all_to_all.19), calls=%async_computation.1 | async-start | bytes 2097152 | tf_op jit(solution)/shard_map/all_to_all | solution.py:113
  157.0 0.6 gather_fusion.1
  157.6 0.2 select_convert_fusion
  157.8 0.5 copy-done.11
  158.3 2.6 %fusion = f32[12,512,64]{1,0,2:T(8,128)S(1)} fusion(f32[12,12,1]{1,0,2:T(8,128)S(1)} %copy-done.11, f32[512,12,64]{0,2,1:T(8,128)S(1)} %bitcast.75, f32[12,64]{0,1:T(8,128)S(1)} %copy.35), kind=kOutput, calls=%fused_computation.3 | convolution fusion | flops 57016320 | bytes 3149376 | tf_op jit(solution)/shard_map/...ab,ca,db->...cd/dot_general | solution.py:32
  160.9 2.5 %fusion.1 = f32[12,512,64]{1,2,0:T(8,128)S(1)} fusion(f32[12,512,64]{1,0,2:T(8,128)S(1)} %fusion), kind=kOutput, calls=%fused_computation.5 | convolution fusion | flops 302133248 | bytes 3145728 | tf_op jit(solution)/shard_map/...ab,ca,db->...cd/dot_general | solution.py:32
  163.4 2.4 %fusion.6 = bf16[1,192,768]{2,1,0:T(8,128)(2,1)} fusion(f32[512,768]{0,1:T(8,128)S(1)} %bitcast.76, s32[]{:T(128)S(6)} %select_n.142), kind=kOutput, calls=%fused_computation.16 | convolution fusion | flops 906264576 | bytes 2260996 | tf_op jit(solution)/shard_map/dot_general | solution.py:123
  165.8 20.6 %all-to-all-done.1 = bf16[128,4,1024]{2,1,0:T(4,128)(2,1)} async-done(((bf16[128,4,1024]{2,1,0:T(4,128)(2,1)}), bf16[128,4,1024]{2,1,0:T(4,128)(2,1)}, u32[]{:S(2)}, u32[]{:S(2)}) %all-to-all-start.1) | async-done | bytes 1048608 | tf_op jit(solution)/shard_map/all_to_all | solution.py:113
  186.4 1.3 all_to_all.21
  187.8 1.2 gather_fusion
  188.9 0.4 fusion.7
  189.3 0.6 add_convert_fusion.1
  (57 shorter events, 1.7 us)
Async XLA Ops:
  0.6 76.3 %copy-start = (bf16[1,192,4096]{2,1,0:T(8,128)(2,1)S(1)}, bf16[1,192,4096]{2,1,0:T(8,128)(2,1)}, u32[]{:S(2)}) copy-start(bf16[1,192,4096]{2,1,0:T(8,128)(2,1)} %param.12) | copy-start | bytes 4718596
  57.0 25.9 %collective-permute-start.2 = (bf16[512,1024]{1,0:T(8,128)(2,1)S(1)}, bf16[512,1024]{1,0:T(8,128)(2,1)}, u32[]{:S(2)}, u32[]{:S(2)}) collective-permute-start(bf16[512,1024]{1,0:T(8,128)(2,1)S(1)} %all_to_all.18), channel_id=1, source_target_pairs={{0,3},{1,0},{2,1},{3,2},{4,7},{5,4},{6,5},{7,6},{8,11},{9,8},{10,9... | collective-permute-start | bytes 3145736 | tf_op jit(solution)/shard_map/ppermute | solution.py:46
  61.5 28.6 %collective-permute-start = (bf16[512,1024]{1,0:T(8,128)(2,1)S(1)}, bf16[512,1024]{1,0:T(8,128)(2,1)}, u32[]{:S(2)}, u32[]{:S(2)}) collective-permute-start(bf16[512,1024]{1,0:T(8,128)(2,1)S(1)} %all_to_all.18), channel_id=1, source_target_pairs={{0,1},{1,2},{2,3},{3,0},{4,5},{5,6},{6,7},{7,4},{8,9},{9,10},{10,1... | collective-permute-start | bytes 3145736 | tf_op jit(solution)/shard_map/ppermute | solution.py:46
  65.7 67.8 %collective-permute-start.4 = (bf16[192,1024]{1,0:T(8,128)(2,1)}, bf16[192,1024]{1,0:T(8,128)(2,1)}, u32[]{:S(2)}, u32[]{:S(2)}) collective-permute-start(bf16[192,1024]{1,0:T(8,128)(2,1)} %get-tuple-element.4), channel_id=1, source_target_pairs={{0,1},{1,2},{2,3},{3,0},{4,5},{5,6},{6,7},{7,4},{8,9},{9,10},{10,1... | collective-permute-start | bytes 1179656 | tf_op jit(solution)/shard_map/ppermute | solution.py:46
  67.8 71.3 %collective-permute-start.6 = (bf16[192,1024]{1,0:T(8,128)(2,1)}, bf16[192,1024]{1,0:T(8,128)(2,1)}, u32[]{:S(2)}, u32[]{:S(2)}) collective-permute-start(bf16[192,1024]{1,0:T(8,128)(2,1)} %get-tuple-element.6), channel_id=1, source_target_pairs={{0,2},{1,3},{2,0},{3,1},{4,6},{5,7},{6,4},{7,5},{8,10},{9,11},{10,... | collective-permute-start | bytes 1179656 | tf_op jit(solution)/shard_map/ppermute | solution.py:46
  73.4 67.3 %collective-permute-start.8 = (bf16[192,1024]{1,0:T(8,128)(2,1)}, bf16[192,1024]{1,0:T(8,128)(2,1)}, u32[]{:S(2)}, u32[]{:S(2)}) collective-permute-start(bf16[192,1024]{1,0:T(8,128)(2,1)} %get-tuple-element.5), channel_id=1, source_target_pairs={{0,3},{1,0},{2,1},{3,2},{4,7},{5,4},{6,5},{7,6},{8,11},{9,8},{10,9... | collective-permute-start | bytes 1179656 | tf_op jit(solution)/shard_map/ppermute | solution.py:46
  76.9 11.4 %copy-start.1 = (bf16[1,192,4096]{2,1,0:T(8,128)(2,1)S(1)}, bf16[1,192,4096]{2,1,0:T(8,128)(2,1)}, u32[]{:S(2)}) copy-start(bf16[1,192,4096]{2,1,0:T(8,128)(2,1)} %param.13) | copy-start | bytes 4718596
  82.9 42.7 %collective-permute-start.1 = (bf16[512,1024]{1,0:T(8,128)(2,1)S(1)}, bf16[512,1024]{1,0:T(8,128)(2,1)S(1)}, u32[]{:S(2)}, u32[]{:S(2)}) collective-permute-start(bf16[512,1024]{1,0:T(8,128)(2,1)S(1)} %all_to_all.18), channel_id=1, source_target_pairs={{0,2},{1,3},{2,0},{3,1},{4,6},{5,7},{6,4},{7,5},{8,10},{9,11},{10,... | collective-permute-start | bytes 3145736 | tf_op jit(solution)/shard_map/ppermute | solution.py:46
  126.7 12.4 %copy-start.2 = (bf16[512,192]{0,1:T(8,128)(2,1)}, bf16[512,192]{0,1:T(8,128)(2,1)S(1)}, u32[]{:S(2)}) copy-start(bf16[512,192]{0,1:T(8,128)(2,1)S(1)} %multiply_convert_fusion) | copy-start | bytes 589828
  126.7 10.8 %collective-permute-start.3 = (bf16[512,192]{0,1:T(8,128)(2,1)S(1)}, bf16[512,192]{0,1:T(8,128)(2,1)S(1)}, u32[]{:S(2)}, u32[]{:S(2)}) collective-permute-start(bf16[512,192]{0,1:T(8,128)(2,1)S(1)} %multiply_convert_fusion), channel_id=1, source_target_pairs={{0,1},{1,2},{2,3},{3,0},{4,5},{5,6},{6,7},{7,4},{8,9},{9,10},{10,1... | collective-permute-start | bytes 589832 | tf_op jit(solution)/shard_map/ppermute | solution.py:46
  128.6 10.4 %collective-permute-start.5 = (bf16[512,192]{0,1:T(8,128)(2,1)S(1)}, bf16[512,192]{0,1:T(8,128)(2,1)S(1)}, u32[]{:S(2)}, u32[]{:S(2)}) collective-permute-start(bf16[512,192]{0,1:T(8,128)(2,1)S(1)} %multiply_convert_fusion), channel_id=1, source_target_pairs={{0,2},{1,3},{2,0},{3,1},{4,6},{5,7},{6,4},{7,5},{8,10},{9,11},{10,... | collective-permute-start | bytes 589832 | tf_op jit(solution)/shard_map/ppermute | solution.py:46
  133.5 8.8 %collective-permute-start.7 = (bf16[512,192]{0,1:T(8,128)(2,1)S(1)}, bf16[512,192]{0,1:T(8,128)(2,1)S(1)}, u32[]{:S(2)}, u32[]{:S(2)}) collective-permute-start(bf16[512,192]{0,1:T(8,128)(2,1)S(1)} %multiply_convert_fusion), channel_id=1, source_target_pairs={{0,3},{1,0},{2,1},{3,2},{4,7},{5,4},{6,5},{7,6},{8,11},{9,8},{10,9... | collective-permute-start | bytes 589832 | tf_op jit(solution)/shard_map/ppermute | solution.py:46
  137.5 3.1 %copy-start.4 = (bf16[512,192]{0,1:T(8,128)(2,1)}, bf16[512,192]{0,1:T(8,128)(2,1)S(1)}, u32[]{:S(2)}) copy-start(bf16[512,192]{0,1:T(8,128)(2,1)S(1)} %collective-permute-done.3) | copy-start | bytes 589828
  139.1 4.7 %copy-start.6 = (bf16[512,192]{0,1:T(8,128)(2,1)}, bf16[512,192]{0,1:T(8,128)(2,1)S(1)}, u32[]{:S(2)}) copy-start(bf16[512,192]{0,1:T(8,128)(2,1)S(1)} %collective-permute-done.5) | copy-start | bytes 589828
  142.3 1.6 copy-start.8
  145.1 11.2 %copy-start.13 = (s32[1,768]{1,0:T(1,128)S(1)}, s32[1,768]{1,0:T(1,128)}, u32[]{:S(2)}) copy-start(s32[1,768]{1,0:T(1,128)} %param.11) | copy-start | bytes 9220
  145.1 11.6 %copy-start.12 = (f32[32,8]{0,1:T(8,128)S(1)}, f32[32,8]{0,1:T(8,128)}, u32[]{:S(2)}) copy-start(f32[32,8]{0,1:T(8,128)} %param.10) | copy-start | bytes 3076
  145.1 11.7 %copy-start.3 = (bf16[512,192]{0,1:T(8,128)(2,1)S(1)}, bf16[512,192]{0,1:T(8,128)(2,1)}, u32[]{:S(2)}) copy-start(bf16[512,192]{0,1:T(8,128)(2,1)} %copy-done.2) | copy-start | bytes 589828
  145.1 11.7 %copy-start.5 = (bf16[512,192]{0,1:T(8,128)(2,1)S(1)}, bf16[512,192]{0,1:T(8,128)(2,1)}, u32[]{:S(2)}) copy-start(bf16[512,192]{0,1:T(8,128)(2,1)} %copy-done.4) | copy-start | bytes 589828
  145.1 11.7 %copy-start.7 = (bf16[512,192]{0,1:T(8,128)(2,1)S(1)}, bf16[512,192]{0,1:T(8,128)(2,1)}, u32[]{:S(2)}) copy-start(bf16[512,192]{0,1:T(8,128)(2,1)} %copy-done.6) | copy-start | bytes 589828
  145.1 11.7 %copy-start.9 = (bf16[512,192]{0,1:T(8,128)(2,1)S(1)}, bf16[512,192]{0,1:T(8,128)(2,1)}, u32[]{:S(2)}) copy-start(bf16[512,192]{0,1:T(8,128)(2,1)} %copy-done.8) | copy-start | bytes 589828
  145.1 41.3 %all-to-all-start.1 = ((bf16[128,4,1024]{2,1,0:T(4,128)(2,1)}), bf16[128,4,1024]{2,1,0:T(4,128)(2,1)}, u32[]{:S(2)}, u32[]{:S(2)}) async-start(bf16[128,4,1024]{2,1,0:T(4,128)(2,1)} %all_to_all.19), calls=%async_computation.1 | async-start | bytes 2097152 | tf_op jit(solution)/shard_map/all_to_all | solution.py:113
  157.6 0.7 copy-start.11
  187.7 1.6 copy-start.10
where the time goes:
time: 191 us; the launch traced here: 190 us
  waiting for transfers between devices  59.8 us (31%)
  blocking collectives  49 us (26%)
  starting transfers between devices  40 us (21%)
  matrix products  24.9 us (13%)
  local copies, waits for them, and re-layouts  11.8 us (6%)
  other arithmetic  3.22 us (2%)
    all_to_all x1, blocking collectives, layer(): lax.all_to_all(sending, 'exp', split_axis=0, concat_axis=0, tiled=True)  49 us
    ppermute x9, waiting for transfers between devices, shift_hid(): lax.ppermute(value, 'hid', [(i, (i + shift) % n_hid) for i in range(n_hid)])  39.2 us
    ppermute x9, starting transfers between devices, shift_hid(): lax.ppermute(value, 'hid', [(i, (i + shift) % n_hid) for i in range(n_hid)])  28.8 us
    all_to_all x1, waiting for transfers between devices, layer(): lax.all_to_all(out_cols, 'exp', split_axis=0, concat_axis=0, tiled=True)  20.6 us
    all_to_all x1, starting transfers between devices, layer(): lax.all_to_all(out_cols, 'exp', split_axis=0, concat_axis=0, tiled=True)  11.2 us
    dot_general x4, matrix products, layer(): jnp.dot(hid_pieces[s], down_pieces[s], preferred_element_type=jnp.float32)  6.07 us
    dot_general x4, matrix products, layer(): jnp.dot(in_pieces[s], lax.dynamic_slice_in_dim(w_up[0], source[s] * own_c...  5.5 us
    dot_general x2, matrix products, rotate(): jnp.einsum('...ab,ca,db->...cd', blocks, paley_table, sylvester_table, pr...  5.09 us
  transfers between devices with their start and end apart: 10, of which 4 were waited for; matrix products, arithmetic and copies ran while one was open for 14% of the time, Pallas kernels for 0%

commit v1 on v0

--- a/solution.py
+++ b/solution.py
@@ -86,9 +86,7 @@
     ).astype(jnp.bfloat16)
     sending = jnp.dot(selector, tokens, preferred_element_type=jnp.float32).astype(jnp.bfloat16)
     arrived = lax.all_to_all(sending, "exp", split_axis=0, concat_axis=0, tiled=True)
-    in_pieces = [arrived]
-    for s in shifts[1:]:
-        in_pieces.append(shift_hid(arrived, s, n_hid))
+    in_pieces = [shift_hid(arrived, s, n_hid) if s else arrived for s in shifts]
     gate_act = sum(
         jnp.dot(
             in_pieces[s],
@@ -110,8 +108,9 @@
     out_cols = sum(
         jnp.dot(hid_pieces[s], down_pieces[s], preferred_element_type=jnp.float32) for s in shifts
     ).astype(jnp.bfloat16)
+    out_cols = out_cols.reshape(n_exp, per_pair, own_cols)
     back_rows = lax.all_to_all(out_cols, "exp", split_axis=0, concat_axis=0, tiled=True)
-    picked = back_rows[target]
+    picked = back_rows[target // per_pair, target % per_pair]
     mixed_rows = tokens.astype(jnp.float32) + jnp.sum(
         combine[:, :, None] * picked.astype(jnp.float32), axis=1
     )

time: 191 us -> 191 us (level)
    all_to_all x2 -> x0, local copies, waits for them, and re-layouts: 2.58 us -> none  [layer(): lax.all_to_all(out_cols, 'exp', split_axis=0, concat_axis=0, tiled=True)]
  transfers between devices with their start and end apart: 10 -> 10, of which waited for: 4 -> 4; matrix products, arithmetic and copies ran while one was open for 14% -> 15% of each run, Pallas kernels for 0% -> 0%
where the time goes in v1:
time: 191 us; the launch traced here: 190 us
  waiting for transfers between devices  58.3 us (31%)
  blocking collectives  49 us (26%)
  starting transfers between devices  39.4 us (21%)
  matrix products  24.7 us (13%)
  local copies, waits for them, and re-layouts  13.2 us (7%)
  other arithmetic  4.17 us (2%)
    all_to_all x1, blocking collectives, layer(): lax.all_to_all(sending, 'exp', split_axis=0, concat_axis=0, tiled=True)  49 us
    ppermute x9, waiting for transfers between devices, shift_hid(): lax.ppermute(value, 'hid', [(i, (i + shift) % n_hid) for i in range(n_hid)])  39.3 us
    ppermute x9, starting transfers between devices, shift_hid(): lax.ppermute(value, 'hid', [(i, (i + shift) % n_hid) for i in range(n_hid)])  28.8 us
    all_to_all x1, waiting for transfers between devices, layer(): lax.all_to_all(out_cols, 'exp', split_axis=0, concat_axis=0, tiled=True)  18.9 us
    all_to_all x1, starting transfers between devices, layer(): lax.all_to_all(out_cols, 'exp', split_axis=0, concat_axis=0, tiled=True)  10.5 us
    dot_general x4, matrix products, layer(): jnp.dot(hid_pieces[s], down_pieces[s], preferred_element_type=jnp.float32)  5.89 us
    dot_general x4, matrix products, layer(): jnp.dot(in_pieces[s], lax.dynamic_slice_in_dim(w_up[0], source[s] * own_c...  5.5 us
    dot_general x2, matrix products, rotate(): jnp.einsum('...ab,ca,db->...cd', blocks, paley_table, sylvester_table, pr...  5.09 us
  transfers between devices with their start and end apart: 10, of which 4 were waited for; matrix products, arithmetic and copies ran while one was open for 15% of the time, Pallas kernels for 0%

profile of v1, /device:TPU:1, one launch (start us, length us, event | category | flops | bytes accessed | tf_op | source)
XLA Modules:
  0.0 189.8 jit_solution(17530303048877348771)
XLA Ops:
  0.7 0.9 fusion.84
  1.8 0.2 reduce_window_sum.17
  2.0 0.2 select_reduce_fusion.1
  2.6 0.2 reduce_window_sum.18
  3.1 0.8 fusion.54
  4.0 0.2 fusion.9
  4.2 1.3 convolution_convert_fusion
  5.5 1.2 all_to_all.11
  6.8 49.0 %all_to_all.17 = bf16[128,4,1024]{2,1,0:T(4,128)(2,1)} all-to-all(bf16[128,4,1024]{2,1,0:T(4,128)(2,1)} %all_to_all.11), channel_id=1, replica_groups=mesh['exp'=128,'hid'=4] {'exp'}, dimensions={0} | all-to-all | bytes 2097152 | tf_op jit(solution)/shard_map/all_to_all | solution.py:88
  55.7 1.3 all_to_all.13
  57.1 4.4 %collective-permute-start.2 = (bf16[512,1024]{1,0:T(8,128)(2,1)S(1)}, bf16[512,1024]{1,0:T(8,128)(2,1)}, u32[]{:S(2)}, u32[]{:S(2)}) collective-permute-start(bf16[512,1024]{1,0:T(8,128)(2,1)S(1)} %all_to_all.13), channel_id=1, source_target_pairs={{0,3},{1,0},{2,1},{3,2},{4,7},{5,4},{6,5},{7,6},{8,11},{9,8},{10,9... | collective-permute-start | bytes 3145736 | tf_op jit(solution)/shard_map/ppermute | solution.py:46
  61.5 1.9 %collective-permute-start = (bf16[512,1024]{1,0:T(8,128)(2,1)S(1)}, bf16[512,1024]{1,0:T(8,128)(2,1)}, u32[]{:S(2)}, u32[]{:S(2)}) collective-permute-start(bf16[512,1024]{1,0:T(8,128)(2,1)S(1)} %all_to_all.13), channel_id=1, source_target_pairs={{0,1},{1,2},{2,3},{3,0},{4,5},{5,6},{6,7},{7,4},{8,9},{9,10},{10,1... | collective-permute-start | bytes 3145736 | tf_op jit(solution)/shard_map/ppermute | solution.py:46
  63.4 2.3 %dynamic-slice_bitcast_fusion.2 = (bf16[192,1024]{1,0:T(8,128)(2,1)}, bf16[192,1024]{1,0:T(8,128)(2,1)}, bf16[192,1024]{1,0:T(8,128)(2,1)}) fusion(bf16[1,192,4096]{2,1,0:T(8,128)(2,1)} %param.14, s32[]{:T(128)S(6)} %select_n.144, s32[]{:T(128)S(6)} %select_n.148, s32[]{:T(128)S(6)} %select_n.146), kind=kLoop, calls=%fused_computation.41 | loop fusion | bytes 2359308 | tf_op jit(solution)/shard_map/dynamic_slice | solution.py:69
  65.8 2.1 %collective-permute-start.4 = (bf16[192,1024]{1,0:T(8,128)(2,1)}, bf16[192,1024]{1,0:T(8,128)(2,1)}, u32[]{:S(2)}, u32[]{:S(2)}) collective-permute-start(bf16[192,1024]{1,0:T(8,128)(2,1)} %get-tuple-element.4), channel_id=1, source_target_pairs={{0,1},{1,2},{2,3},{3,0},{4,5},{5,6},{6,7},{7,4},{8,9},{9,10},{10,1... | collective-permute-start | bytes 1179656 | tf_op jit(solution)/shard_map/ppermute | solution.py:46
  67.8 5.6 %collective-permute-start.6 = (bf16[192,1024]{1,0:T(8,128)(2,1)}, bf16[192,1024]{1,0:T(8,128)(2,1)}, u32[]{:S(2)}, u32[]{:S(2)}) collective-permute-start(bf16[192,1024]{1,0:T(8,128)(2,1)} %get-tuple-element.6), channel_id=1, source_target_pairs={{0,2},{1,3},{2,0},{3,1},{4,6},{5,7},{6,4},{7,5},{8,10},{9,11},{10,... | collective-permute-start | bytes 1179656 | tf_op jit(solution)/shard_map/ppermute | solution.py:46
  73.4 1.9 %collective-permute-start.8 = (bf16[192,1024]{1,0:T(8,128)(2,1)}, bf16[192,1024]{1,0:T(8,128)(2,1)}, u32[]{:S(2)}, u32[]{:S(2)}) collective-permute-start(bf16[192,1024]{1,0:T(8,128)(2,1)} %get-tuple-element.5), channel_id=1, source_target_pairs={{0,3},{1,0},{2,1},{3,2},{4,7},{5,4},{6,5},{7,6},{8,11},{9,8},{10,9... | collective-permute-start | bytes 1179656 | tf_op jit(solution)/shard_map/ppermute | solution.py:46
  75.4 1.5 fusion.16
  77.0 0.5 fusion.22
  77.5 5.5 %collective-permute-done.2 = bf16[512,1024]{1,0:T(8,128)(2,1)} collective-permute-done((bf16[512,1024]{1,0:T(8,128)(2,1)S(1)}, bf16[512,1024]{1,0:T(8,128)(2,1)}, u32[]{:S(2)}, u32[]{:S(2)}) %collective-permute-start.2) | collective-permute-done | bytes 1048608 | tf_op jit(solution)/shard_map/ppermute | solution.py:46
  83.0 3.7 %collective-permute-start.1 = (bf16[512,1024]{1,0:T(8,128)(2,1)S(1)}, bf16[512,1024]{1,0:T(8,128)(2,1)S(1)}, u32[]{:S(2)}, u32[]{:S(2)}) collective-permute-start(bf16[512,1024]{1,0:T(8,128)(2,1)S(1)} %all_to_all.13), channel_id=1, source_target_pairs={{0,2},{1,3},{2,0},{3,1},{4,6},{5,7},{6,4},{7,5},{8,10},{9,11},{10,... | collective-permute-start | bytes 3145736 | tf_op jit(solution)/shard_map/ppermute | solution.py:46
  86.6 1.7 fusion.18
  88.4 1.7 fusion.12
  90.1 1.7 convolution_add_fusion.1
  91.9 1.7 convolution_add_fusion.3
  93.6 32.1 %collective-permute-done.1 = bf16[512,1024]{1,0:T(8,128)(2,1)S(1)} collective-permute-done((bf16[512,1024]{1,0:T(8,128)(2,1)S(1)}, bf16[512,1024]{1,0:T(8,128)(2,1)S(1)}, u32[]{:S(2)}, u32[]{:S(2)}) %collective-permute-start.1) | collective-permute-done | bytes 1048608 | tf_op jit(solution)/shard_map/ppermute | solution.py:46
  125.7 0.5 fusion.4
  126.2 0.5 multiply_convert_fusion
  126.7 1.9 %collective-permute-start.3 = (bf16[512,192]{0,1:T(8,128)(2,1)S(1)}, bf16[512,192]{0,1:T(8,128)(2,1)S(1)}, u32[]{:S(2)}, u32[]{:S(2)}) collective-permute-start(bf16[512,192]{0,1:T(8,128)(2,1)S(1)} %multiply_convert_fusion), channel_id=1, source_target_pairs={{0,1},{1,2},{2,3},{3,0},{4,5},{5,6},{6,7},{7,4},{8,9},{9,10},{10,1... | collective-permute-start | bytes 589832 | tf_op jit(solution)/shard_map/ppermute | solution.py:46
  128.7 3.4 %collective-permute-start.5 = (bf16[512,192]{0,1:T(8,128)(2,1)S(1)}, bf16[512,192]{0,1:T(8,128)(2,1)S(1)}, u32[]{:S(2)}, u32[]{:S(2)}) collective-permute-start(bf16[512,192]{0,1:T(8,128)(2,1)S(1)} %multiply_convert_fusion), channel_id=1, source_target_pairs={{0,2},{1,3},{2,0},{3,1},{4,6},{5,7},{6,4},{7,5},{8,10},{9,11},{10,... | collective-permute-start | bytes 589832 | tf_op jit(solution)/shard_map/ppermute | solution.py:46
  132.1 1.5 fusion.10
  133.5 4.0 %collective-permute-start.7 = (bf16[512,192]{0,1:T(8,128)(2,1)S(1)}, bf16[512,192]{0,1:T(8,128)(2,1)S(1)}, u32[]{:S(2)}, u32[]{:S(2)}) collective-permute-start(bf16[512,192]{0,1:T(8,128)(2,1)S(1)} %multiply_convert_fusion), channel_id=1, source_target_pairs={{0,3},{1,0},{2,1},{3,2},{4,7},{5,4},{6,5},{7,6},{8,11},{9,8},{10,9... | collective-permute-start | bytes 589832 | tf_op jit(solution)/shard_map/ppermute | solution.py:46
  137.5 1.5 fusion.85
  139.0 1.5 fusion.86
  140.5 1.8 collective-permute-done.7
  142.3 1.5 add_convert_fusion
  143.8 1.2 reshape.115
  145.0 10.5 %all-to-all-start.1 = ((bf16[128,4,1024]{2,1,0:T(4,128)(2,1)}), bf16[128,4,1024]{2,1,0:T(4,128)(2,1)S(1)}, u32[]{:S(2)}, u32[]{:S(2)}) async-start(bf16[128,4,1024]{2,1,0:T(4,128)(2,1)} %reshape.115), calls=%async_computation.1 | async-start | bytes 2097152 | tf_op jit(solution)/shard_map/all_to_all | solution.py:112
  156.1 1.0 pad_maximum_fusion
  157.1 1.7 gather_fusion.1
  158.8 0.2 select_convert_fusion
  159.0 0.5 copy-done.3
  159.5 2.6 %fusion = f32[12,512,64]{1,0,2:T(8,128)S(1)} fusion(f32[12,12,1]{1,0,2:T(8,128)S(1)} %copy-done.3, f32[512,12,64]{0,2,1:T(8,128)S(1)} %bitcast.75, f32[12,64]{0,1:T(8,128)S(1)} %copy.35), kind=kOutput, calls=%fused_computation.3 | convolution fusion | flops 57016320 | bytes 3149376 | tf_op jit(solution)/shard_map/...ab,ca,db->...cd/dot_general | solution.py:32
  162.1 2.5 %fusion.1 = f32[12,512,64]{1,2,0:T(8,128)S(1)} fusion(f32[12,512,64]{1,0,2:T(8,128)S(1)} %fusion), kind=kOutput, calls=%fused_computation.5 | convolution fusion | flops 302133248 | bytes 3145728 | tf_op jit(solution)/shard_map/...ab,ca,db->...cd/dot_general | solution.py:32
  164.6 2.4 %fusion.6 = bf16[1,192,768]{2,1,0:T(8,128)(2,1)} fusion(f32[512,768]{0,1:T(8,128)S(1)} %bitcast.76, s32[]{:T(128)S(6)} %select_n.159), kind=kOutput, calls=%fused_computation.16 | convolution fusion | flops 906264576 | bytes 2260996 | tf_op jit(solution)/shard_map/dot_general | solution.py:122
  167.1 18.9 %all-to-all-done.1 = bf16[128,4,1024]{2,1,0:T(4,128)(2,1)S(1)} async-done(((bf16[128,4,1024]{2,1,0:T(4,128)(2,1)}), bf16[128,4,1024]{2,1,0:T(4,128)(2,1)S(1)}, u32[]{:S(2)}, u32[]{:S(2)}) %all-to-all-start.1) | async-done | bytes 1048608 | tf_op jit(solution)/shard_map/all_to_all | solution.py:112
  186.0 2.8 %gather_fusion = bf16[256,1024]{1,0:T(8,128)(2,1)S(1)} fusion(bf16[128,4,1024]{2,1,0:T(4,128)(2,1)S(1)} %all-to-all-done.1, s32[256]{0:T(256)S(1)} %reshape.118), kind=kCustom, calls=%fused_computation | custom fusion | bytes 1050624 | tf_op jit(solution)/shard_map/gather | solution.py:113
  188.8 0.4 fusion.7
  189.2 0.6 add_convert_fusion.1
  (39 shorter events, 1.6 us)
Async XLA Ops:
  0.6 76.3 %copy-start = (bf16[1,192,4096]{2,1,0:T(8,128)(2,1)S(1)}, bf16[1,192,4096]{2,1,0:T(8,128)(2,1)}, u32[]{:S(2)}) copy-start(bf16[1,192,4096]{2,1,0:T(8,128)(2,1)} %param.12) | copy-start | bytes 4718596
  57.1 25.9 %collective-permute-start.2 = (bf16[512,1024]{1,0:T(8,128)(2,1)S(1)}, bf16[512,1024]{1,0:T(8,128)(2,1)}, u32[]{:S(2)}, u32[]{:S(2)}) collective-permute-start(bf16[512,1024]{1,0:T(8,128)(2,1)S(1)} %all_to_all.13), channel_id=1, source_target_pairs={{0,3},{1,0},{2,1},{3,2},{4,7},{5,4},{6,5},{7,6},{8,11},{9,8},{10,9... | collective-permute-start | bytes 3145736 | tf_op jit(solution)/shard_map/ppermute | solution.py:46
  61.5 28.6 %collective-permute-start = (bf16[512,1024]{1,0:T(8,128)(2,1)S(1)}, bf16[512,1024]{1,0:T(8,128)(2,1)}, u32[]{:S(2)}, u32[]{:S(2)}) collective-permute-start(bf16[512,1024]{1,0:T(8,128)(2,1)S(1)} %all_to_all.13), channel_id=1, source_target_pairs={{0,1},{1,2},{2,3},{3,0},{4,5},{5,6},{6,7},{7,4},{8,9},{9,10},{10,1... | collective-permute-start | bytes 3145736 | tf_op jit(solution)/shard_map/ppermute | solution.py:46
  65.8 67.8 %collective-permute-start.4 = (bf16[192,1024]{1,0:T(8,128)(2,1)}, bf16[192,1024]{1,0:T(8,128)(2,1)}, u32[]{:S(2)}, u32[]{:S(2)}) collective-permute-start(bf16[192,1024]{1,0:T(8,128)(2,1)} %get-tuple-element.4), channel_id=1, source_target_pairs={{0,1},{1,2},{2,3},{3,0},{4,5},{5,6},{6,7},{7,4},{8,9},{9,10},{10,1... | collective-permute-start | bytes 1179656 | tf_op jit(solution)/shard_map/ppermute | solution.py:46
  67.8 71.2 %collective-permute-start.6 = (bf16[192,1024]{1,0:T(8,128)(2,1)}, bf16[192,1024]{1,0:T(8,128)(2,1)}, u32[]{:S(2)}, u32[]{:S(2)}) collective-permute-start(bf16[192,1024]{1,0:T(8,128)(2,1)} %get-tuple-element.6), channel_id=1, source_target_pairs={{0,2},{1,3},{2,0},{3,1},{4,6},{5,7},{6,4},{7,5},{8,10},{9,11},{10,... | collective-permute-start | bytes 1179656 | tf_op jit(solution)/shard_map/ppermute | solution.py:46
  73.4 67.1 %collective-permute-start.8 = (bf16[192,1024]{1,0:T(8,128)(2,1)}, bf16[192,1024]{1,0:T(8,128)(2,1)}, u32[]{:S(2)}, u32[]{:S(2)}) collective-permute-start(bf16[192,1024]{1,0:T(8,128)(2,1)} %get-tuple-element.5), channel_id=1, source_target_pairs={{0,3},{1,0},{2,1},{3,2},{4,7},{5,4},{6,5},{7,6},{8,11},{9,8},{10,9... | collective-permute-start | bytes 1179656 | tf_op jit(solution)/shard_map/ppermute | solution.py:46
  77.0 11.4 %copy-start.1 = (bf16[1,192,4096]{2,1,0:T(8,128)(2,1)S(1)}, bf16[1,192,4096]{2,1,0:T(8,128)(2,1)}, u32[]{:S(2)}) copy-start(bf16[1,192,4096]{2,1,0:T(8,128)(2,1)} %param.13) | copy-start | bytes 4718596
  83.0 42.7 %collective-permute-start.1 = (bf16[512,1024]{1,0:T(8,128)(2,1)S(1)}, bf16[512,1024]{1,0:T(8,128)(2,1)S(1)}, u32[]{:S(2)}, u32[]{:S(2)}) collective-permute-start(bf16[512,1024]{1,0:T(8,128)(2,1)S(1)} %all_to_all.13), channel_id=1, source_target_pairs={{0,2},{1,3},{2,0},{3,1},{4,6},{5,7},{6,4},{7,5},{8,10},{9,11},{10,... | collective-permute-start | bytes 3145736 | tf_op jit(solution)/shard_map/ppermute | solution.py:46
  126.7 10.8 %collective-permute-start.3 = (bf16[512,192]{0,1:T(8,128)(2,1)S(1)}, bf16[512,192]{0,1:T(8,128)(2,1)S(1)}, u32[]{:S(2)}, u32[]{:S(2)}) collective-permute-start(bf16[512,192]{0,1:T(8,128)(2,1)S(1)} %multiply_convert_fusion), channel_id=1, source_target_pairs={{0,1},{1,2},{2,3},{3,0},{4,5},{5,6},{6,7},{7,4},{8,9},{9,10},{10,1... | collective-permute-start | bytes 589832 | tf_op jit(solution)/shard_map/ppermute | solution.py:46
  128.7 10.4 %collective-permute-start.5 = (bf16[512,192]{0,1:T(8,128)(2,1)S(1)}, bf16[512,192]{0,1:T(8,128)(2,1)S(1)}, u32[]{:S(2)}, u32[]{:S(2)}) collective-permute-start(bf16[512,192]{0,1:T(8,128)(2,1)S(1)} %multiply_convert_fusion), channel_id=1, source_target_pairs={{0,2},{1,3},{2,0},{3,1},{4,6},{5,7},{6,4},{7,5},{8,10},{9,11},{10,... | collective-permute-start | bytes 589832 | tf_op jit(solution)/shard_map/ppermute | solution.py:46
  133.5 8.8 %collective-permute-start.7 = (bf16[512,192]{0,1:T(8,128)(2,1)S(1)}, bf16[512,192]{0,1:T(8,128)(2,1)S(1)}, u32[]{:S(2)}, u32[]{:S(2)}) collective-permute-start(bf16[512,192]{0,1:T(8,128)(2,1)S(1)} %multiply_convert_fusion), channel_id=1, source_target_pairs={{0,3},{1,0},{2,1},{3,2},{4,7},{5,4},{6,5},{7,6},{8,11},{9,8},{10,9... | collective-permute-start | bytes 589832 | tf_op jit(solution)/shard_map/ppermute | solution.py:46
  145.0 10.6 %copy-start.5 = (s32[1,768]{1,0:T(1,128)S(1)}, s32[1,768]{1,0:T(1,128)}, u32[]{:S(2)}) copy-start(s32[1,768]{1,0:T(1,128)} %param.11) | copy-start | bytes 9220
  145.0 10.9 %copy-start.4 = (f32[32,8]{0,1:T(8,128)S(1)}, f32[32,8]{0,1:T(8,128)}, u32[]{:S(2)}) copy-start(f32[32,8]{0,1:T(8,128)} %param.10) | copy-start | bytes 3076
  145.0 41.0 %all-to-all-start.1 = ((bf16[128,4,1024]{2,1,0:T(4,128)(2,1)}), bf16[128,4,1024]{2,1,0:T(4,128)(2,1)S(1)}, u32[]{:S(2)}, u32[]{:S(2)}) async-start(bf16[128,4,1024]{2,1,0:T(4,128)(2,1)} %reshape.115), calls=%async_computation.1 | async-start | bytes 2097152 | tf_op jit(solution)/shard_map/all_to_all | solution.py:112
  158.8 0.7 copy-start.3
  167.1 22.1 %copy-start.2 = (bf16[32,1024]{1,0:T(8,128)(2,1)S(1)}, bf16[32,1024]{1,0:T(8,128)(2,1)}, u32[]{:S(2)}) copy-start(bf16[32,1024]{1,0:T(8,128)(2,1)} %param.8) | copy-start | bytes 196612
